TPU v7x, 512 devices: a whole 4x8x8 slice. The times are simulated.
512 devices in a mesh: dp: 16 (over y, core), tensor: 32 (over z, x).
Axes of the slice: x: 4, y: 8, z: 8, core: 2. Of those that a mesh axis runs over, the one named last changes fastest.
Arguments:
- layer_input: bfloat16 [65536, 8192], P('dp', 'tensor'), may hold values from -6 to 6
- output_grad: bfloat16 [65536, 1024], P(('dp', 'tensor')), may hold values from -6 to 6
- key_weight: bfloat16 [8192, 1024], P('tensor'), may hold values from -0.0625 to 0.0625
- adapter_down: bfloat16 [128, 16, 8192], P('dp', None, 'tensor'), may hold values from -0.0625 to 0.0625
- adapter_up: bfloat16 [128, 16, 1024], P('dp', None, 'tensor'), may hold values from -0.1875 to 0.1875
- segment_adapter: int32 [512], replicated, may hold values from 0 to 127
- adapter_slot: int32 [128], replicated, may hold values from 0 to 127, each once
- live_segments: int32 [16], P('dp'), may hold values from 1 to 32, as said below
Outputs:
- input_grad: bfloat16 [65536, 8192], P('dp', 'tensor')
- down_grad: bfloat16 [128, 16, 8192], P('dp', None, 'tensor')
- up_grad: bfloat16 [128, 16, 1024], P('dp', None, 'tensor')
Inputs may be any that keep to these rules, and one draw needn't show every extreme that they name: `live_segments`: some data group has all 32 segments live; a group's segments at or past its count are padding.
All inputs are finite; a program needn't handle non-finite values.
Results may differ from a plain program's by a relative error of at most 0.0057.
Values may be sent and summed in bfloat16 or wider, within the bound.
No kernel may reach another device: no remote copies, remote signals or barrier semaphores. Data moves between devices by JAX's collectives and lax.ppermute only.
A program may use at most 64 MiB of HBM per device.

v0:
```python
import jax
import jax.numpy as jnp
from jax import lax
from jax.sharding import PartitionSpec as P


def on_device(
    layer_input,
    output_grad,
    key_weight,
    adapter_down,
    adapter_up,
    segment_adapter,
    adapter_slot,
    live_segments,
):
    tensor_size = lax.axis_size("tensor")
    position = lax.axis_index("tensor")
    group_count = lax.axis_size("dp")
    group_index = lax.axis_index("dp")
    row_count = output_grad.shape[0]
    tok_group = layer_input.shape[0]
    width_shard = layer_input.shape[1]
    key_width = output_grad.shape[1]
    key_shard = key_width // tensor_size
    adapters = adapter_slot.shape[0]
    rank_dim = adapter_down.shape[1]
    seg_total = segment_adapter.shape[0]
    seg_group = seg_total // group_count
    seg_len = tok_group // seg_group
    per_owner = adapters // group_count
    slot_ids = jnp.arange(adapters, dtype=jnp.int32)
    lookup = segment_adapter[:, None] == slot_ids[None, :]
    every_slot = jnp.sum(jnp.where(lookup, adapter_slot[None, :], 0), axis=1)
    seg_slot = lax.dynamic_slice_in_dim(every_slot, group_index * seg_group, seg_group)
    local_rows = position * row_count + jnp.arange(row_count, dtype=jnp.int32)
    live_rows = local_rows // seg_len < live_segments[0]
    masked = jnp.where(live_rows[:, None], output_grad, jnp.zeros_like(output_grad))
    whole = lax.all_gather(masked, "tensor", axis=0, tiled=True)
    stores = (
        lax.all_gather(adapter_down, "dp", axis=0, tiled=True),
        lax.all_gather(adapter_up, "dp", axis=0, tiled=True),
    )
    choose = (seg_slot[:, None] == slot_ids[None, :]).astype(jnp.bfloat16)
    down_seg = jnp.dot(choose, stores[0].reshape(adapters, -1), preferred_element_type=jnp.float32)
    down_seg = down_seg.astype(jnp.bfloat16).reshape(seg_group, rank_dim, width_shard)
    up_seg = jnp.dot(choose, stores[1].reshape(adapters, -1), preferred_element_type=jnp.float32)
    up_seg = up_seg.astype(jnp.bfloat16).reshape(seg_group, rank_dim, key_shard)
    own_keys = lax.dynamic_slice_in_dim(whole, position * key_shard, key_shard, 1).reshape(
        seg_group, seg_len, key_shard
    )
    input_seg = layer_input.reshape(seg_group, seg_len, width_shard)
    up_part = jnp.einsum("sjk,srk->rsj", own_keys, up_seg, preferred_element_type=jnp.float32)
    down_part = jnp.einsum("sjd,srd->rsj", input_seg, down_seg, preferred_element_type=jnp.float32)
    lowrank, projected = lax.psum((up_part, down_part), "tensor")
    lowrank = lowrank.astype(jnp.bfloat16)
    projected = projected.astype(jnp.bfloat16)
    frozen = lax.dot_general(
        whole, key_weight, (((1,), (1,)), ((), ())), preferred_element_type=jnp.float32
    )
    extra = jnp.einsum("rsj,srd->sjd", lowrank, down_seg, preferred_element_type=jnp.float32)
    input_grad = (frozen + 2.0 * extra.reshape(tok_group, width_shard)).astype(jnp.bfloat16)
    seg_down = 2.0 * jnp.einsum(
        "rsj,sjd->srd", lowrank, input_seg, preferred_element_type=jnp.float32
    )
    seg_up = 2.0 * jnp.einsum(
        "rsj,sjk->srk", projected, own_keys, preferred_element_type=jnp.float32
    )
    seg_index = jnp.arange(seg_group, dtype=jnp.int32)
    same = seg_slot[:, None] == seg_slot[None, :]
    earlier = same & (seg_index[None, :] < seg_index[:, None])
    leading = jnp.logical_not(jnp.any(earlier, axis=1))
    merge_rows = (same & leading[:, None]).astype(jnp.float32)
    rows_down = jnp.einsum(
        "us,srd->urd", merge_rows, seg_down, precision=lax.Precision.HIGHEST
    ).astype(jnp.bfloat16)
    rows_up = jnp.einsum("us,srk->urk", merge_rows, seg_up, precision=lax.Precision.HIGHEST).astype(
        jnp.bfloat16
    )
    every_down, every_up = (
        lax.all_gather(rows_down, "dp", axis=0, tiled=True),
        lax.all_gather(rows_up, "dp", axis=0, tiled=True),
    )
    owned = group_index * per_owner + jnp.arange(per_owner, dtype=jnp.int32)
    mine = (every_slot[:, None] == owned[None, :]).astype(jnp.bfloat16)
    down_grad = jnp.einsum(
        "sp,srd->prd", mine, every_down, preferred_element_type=jnp.float32
    ).astype(jnp.bfloat16)
    up_grad = jnp.einsum("sp,srk->prk", mine, every_up, preferred_element_type=jnp.float32).astype(
        jnp.bfloat16
    )
    return (input_grad, down_grad, up_grad)


def solution(mesh):
    in_specs = (
        P("dp", "tensor"),
        P(("dp", "tensor"), None),
        P("tensor", None),
        P("dp", None, "tensor"),
        P("dp", None, "tensor"),
        P(),
        P(),
        P("dp"),
    )
    out_specs = (P("dp", "tensor"), P("dp", None, "tensor"), P("dp", None, "tensor"))
    return jax.shard_map(
        on_device, mesh=mesh, in_specs=in_specs, out_specs=out_specs, check_vma=False
    )
```

profile of v0, /device:TPU:1, one launch (start us, length us, event | category | flops | bytes accessed | tf_op | source)
XLA Modules:
  0.0 368.9 jit_solution(6331386676512770924)
XLA Ops:
  7.2 0.0 copy-start
  7.2 0.0 all-gather.6.cloned.1.call-start
  7.2 0.7 all-gather.6.cloned.1.call-update
  7.9 0.0 all-gather.4.cloned.1.call-start
  8.6 1.7 broadcast_select_fusion
  10.4 0.0 all-gather.4.cloned.1.call-update
  10.4 0.0 all-gather.8.cloned.1.call-start
  10.5 0.9 select_reduce_fusion
  11.4 0.1 dynamic_slice.6
  11.5 0.2 fusion.6
  11.7 22.9 %all_gather.16 = bf16[128,16,32]{2,1,0:T(8,128)(2,1)S(1)} all-gather(bf16[8,16,32]{2,1,0:T(8,128)(2,1)} %param.12), channel_id=1, replica_groups=mesh['dp'=16,'tensor'=32] {'dp'}, dimensions={0}, use_global_device_ids=true | all-gather | bytes 139264 | tf_op jit(solution)/shard_map/all_gather | solution.py:42
  34.5 0.4 copy.26
  35.0 0.2 convolution_convert_fusion.5
  35.1 0.2 reshape.60
  35.3 21.6 %all-gather.6.cloned.1.call-done = bf16[128,16,256]{2,1,0:T(8,128)(2,1)} async-done(((bf16[8,16,256]{2,1,0:T(8,128)(2,1)}), bf16[128,16,256]{2,1,0:T(8,128)(2,1)}) %all-gather.6.cloned.1.call-update) | async-done | bytes 1048592 | tf_op jit(solution)/shard_map/all_gather | solution.py:41
  56.9 1.6 copy.37
  58.5 0.3 convolution_convert_fusion
  58.8 0.1 copy.38
  58.9 0.0 copy-done
  58.9 1.4 convolution_bitcast_fusion
  60.3 103.2 %all-gather.4.cloned.1.call-done = bf16[4096,1024]{1,0:T(8,128)(2,1)} async-done(((bf16[128,1024]{1,0:T(8,128)(2,1)}), bf16[4096,1024]{1,0:T(8,128)(2,1)}) %all-gather.4.cloned.1.call-update) | async-done | bytes 8388624 | tf_op jit(solution)/shard_map/all_gather | solution.py:39
  163.5 1.6 constant_dynamic-slice_fusion
  165.0 1.4 convolution_bitcast_fusion.1
  166.4 117.5 %all-reduce.2 = (bf16[16,32,128]{2,0,1:T(8,128)(2,1)S(1)}, bf16[16,32,128]{2,0,1:T(8,128)(2,1)}) all-reduce(f32[16,32,128]{2,0,1:T(8,128)} %convolution_bitcast_fusion.1, f32[16,32,128]{2,0,1:T(8,128)} %convolution_bitcast_fusion), channel_id=1, replica_groups=mesh['dp'=16,'tensor'=32] {'tensor'}, use_global_device_ids=true, to_apply=%region_1.2 | all-reduce | flops 131072 | bytes 786432 | tf_op jit(solution)/shard_map/psum | solution.py:55
  283.9 0.4 convolution_multiply_fusion.1
  284.3 1.4 convolution_convert_fusion.1
  285.7 0.0 all-gather.8.cloned.1.call-update
  285.8 1.3 convolution_multiply_fusion.2
  287.0 0.4 convolution_convert_fusion.2
  287.4 0.0 copy-start.1
  287.4 57.7 %all_gather.19 = bf16[512,16,32]{2,0,1:T(8,128)(2,1)S(1)} all-gather(bf16[32,16,32]{2,0,1:T(8,128)(2,1)S(1)} %convolution_convert_fusion.2), channel_id=1, replica_groups=mesh['dp'=16,'tensor'=32] {'dp'}, dimensions={0}, use_global_device_ids=true | all-gather | bytes 557056 | tf_op jit(solution)/shard_map/all_gather | solution.py:82
  345.1 0.4 convolution_convert_fusion.4
  345.5 0.6 copy.33
  346.2 0.8 convolution_multiply_fusion
  346.9 0.0 copy-done.1
  346.9 7.5 %fusion = bf16[4096,256]{1,0:T(8,128)(2,1)} fusion(f32[4096,256]{1,0:T(8,128)S(1)} %bitcast.43, bf16[4096,1024]{1,0:T(8,128)(2,1)} %all-gather.4.cloned.1.call-done, bf16[256,1024]{1,0:T(8,128)(2,1)S(1)} %copy-done.1), kind=kOutput, calls=%fused_computation.1 | convolution fusion | flops 2149580800 | bytes 15204352 | tf_op jit(solution)/shard_map/dot_general | solution.py:58
  354.4 4.4 %all-gather.8.cloned.1.call-done = bf16[512,16,256]{2,0,1:T(8,128)(2,1)} async-done(((bf16[32,16,256]{2,0,1:T(8,128)(2,1)}), bf16[512,16,256]{2,0,1:T(8,128)(2,1)}) %all-gather.8.cloned.1.call-update) | async-done | bytes 4194320 | tf_op jit(solution)/shard_map/all_gather | solution.py:81
  358.9 2.9 convolution_convert_fusion.3
  361.7 0.7 copy.32
  (3 shorter events, 0.0 us)
Async XLA Ops:
  7.2 51.7 %copy-start = (bf16[4096,256]{1,0:T(8,128)(2,1)S(1)}, bf16[4096,256]{1,0:T(8,128)(2,1)}, u32[]{:S(2)}) copy-start(bf16[4096,256]{1,0:T(8,128)(2,1)} %param.8) | copy-start | bytes 6291460
  7.2 49.7 %all-gather.6.cloned.1.call-start = ((), (), s32[]{:S(2)}) async-start(), calls=%async_computation.1 | async-start | bytes 1114112 | tf_op jit(solution)/shard_map/all_gather | solution.py:41
  7.9 155.5 %all-gather.4.cloned.1.call-start = ((), (), s32[]{:S(2)}) async-start(), calls=%async_computation | async-start | bytes 8650752 | tf_op jit(solution)/shard_map/all_gather | solution.py:39
  10.4 348.5 %all-gather.8.cloned.1.call-start = ((), (), s32[]{:S(2)}) async-start(), calls=%async_computation.2 | async-start | bytes 4456448 | tf_op jit(solution)/shard_map/all_gather | solution.py:81
  287.4 59.5 %copy-start.1 = (bf16[256,1024]{1,0:T(8,128)(2,1)S(1)}, bf16[256,1024]{1,0:T(8,128)(2,1)}, u32[]{:S(2)}) copy-start(bf16[256,1024]{1,0:T(8,128)(2,1)} %param.10) | copy-start | bytes 1572868
Sparse Core Ops, SparseCore 0:
  10.1 46.6 all-gather.5
  60.6 102.8 all-gather.3
  285.9 72.9 all-gather.7
where the time goes:
time: 369 us
  blocking collectives  198 us (54%)
  waiting for transfers between devices  130 us (35%)
  matrix products  18.2 us (5%)
  between operations  14.5 us (4%)
  local copies, waits for them, and re-layouts  5.25 us (1%)
    psum x1, blocking collectives, on_device(): lowrank, projected = lax.psum((up_part, down_part), 'tensor')  117 us
    all_gather x1, waiting for transfers between devices, on_device(): whole = lax.all_gather(masked, 'tensor', axis=0, tiled=True)  103 us
    all_gather x1, blocking collectives, on_device(): lax.all_gather(rows_up, 'dp', axis=0, tiled=True)  57.7 us
    all_gather x1, blocking collectives, on_device(): lax.all_gather(adapter_up, 'dp', axis=0, tiled=True)  22.9 us
    all_gather x1, waiting for transfers between devices, on_device(): lax.all_gather(adapter_down, 'dp', axis=0, tiled=True)  21.6 us
    dot_general x1, matrix products, on_device(): lax.dot_general(whole, key_weight, (((1,), (1,)), ((), ())), preferred_el...  7.47 us
  transfers between devices with their start and end apart: 3, of which 3 were waited for; matrix products, arithmetic and copies ran while one was open for 5% of the time, Pallas kernels for 0%

commit v1 on v0

--- a/solution.py
+++ b/solution.py
@@ -2,6 +2,22 @@
 import jax.numpy as jnp
 from jax import lax
 from jax.sharding import PartitionSpec as P
+
+
+def ring_gather(x, axis, dim):
+    ways, here, step = (lax.axis_size(axis), lax.axis_index(axis), x.shape[dim])
+    lengths = [n * ways if d == dim else n for d, n in enumerate(x.shape)]
+    full = lax.dynamic_update_slice_in_dim(jnp.zeros(lengths, x.dtype), x, here * step, axis=dim)
+    going_up = going_down = x
+    for far in range(1, ways // 2 + 1):
+        going_up = lax.ppermute(going_up, axis, [(d, (d + 1) % ways) for d in range(ways)])
+        full = lax.dynamic_update_slice_in_dim(full, going_up, (here - far) % ways * step, axis=dim)
+        if 2 * far < ways:
+            going_down = lax.ppermute(going_down, axis, [(d, (d - 1) % ways) for d in range(ways)])
+            full = lax.dynamic_update_slice_in_dim(
+                full, going_down, (here + far) % ways * step, axis=dim
+            )
+    return full
 
 
 def on_device(
@@ -79,7 +95,7 @@
     )
     every_down, every_up = (
         lax.all_gather(rows_down, "dp", axis=0, tiled=True),
-        lax.all_gather(rows_up, "dp", axis=0, tiled=True),
+        ring_gather(rows_up, "dp", 0),
     )
     owned = group_index * per_owner + jnp.arange(per_owner, dtype=jnp.int32)
     mine = (every_slot[:, None] == owned[None, :]).astype(jnp.bfloat16)

time: 369 us -> 429 us (1.16); the launches traced: 369 us -> 422 us
  blocking collectives: 198 us -> 141 us
  local copies, waits for them, and re-layouts: 5.25 us -> 50.6 us
  starting transfers between devices: 0.12 us -> 42.9 us
  waiting for transfers between devices: 130 us -> 152 us
    all_gather x1 -> x0, blocking collectives: 57.7 us -> none  [on_device(): lax.all_gather(rows_up, 'dp', axis=0, tiled=True)]
    dynamic_update_slice x0 -> x16, local copies, waits for them, and re-layouts: none -> 44 us  [the longest x8 21.6 us: ring_gather(): lax.dynamic_update_slice_in_dim(full, going_up, (here - far) % ways * ste...]
    ppermute x0 -> x15, starting transfers between devices: none -> 42.8 us  [the longest x8 39 us: ring_gather(): lax.ppermute(going_up, axis, [(d, (d + 1) % ways) for d in range(ways)])]
    ppermute x0 -> x15, waiting for transfers between devices: none -> 26.6 us  [the longest x7 20.2 us: ring_gather(): lax.ppermute(going_down, axis, [(d, (d - 1) % ways) for d in range(ways)])]
    all_gather x1, waiting for transfers between devices: 4.45 us -> 0.01 us  [on_device(): lax.all_gather(rows_down, 'dp', axis=0, tiled=True)]
  transfers between devices with their start and end apart: 3 -> 18, of which waited for: 3 -> 14; matrix products, arithmetic and copies ran while one was open for 5% -> 15% of each run, Pallas kernels for 0% -> 0%
where the time goes in v1:
time: 429 us; the launch traced here: 422 us
  waiting for transfers between devices  152 us (35%)
  blocking collectives  141 us (33%)
  local copies, waits for them, and re-layouts  50.6 us (12%)
  starting transfers between devices  42.9 us (10%)
  matrix products  18.8 us (4%)
  between operations  14.7 us (3%)
    psum x1, blocking collectives, on_device(): lowrank, projected = lax.psum((up_part, down_part), 'tensor')  118 us
    all_gather x1, waiting for transfers between devices, on_device(): whole = lax.all_gather(masked, 'tensor', axis=0, tiled=True)  103 us
    ppermute x8, starting transfers between devices, ring_gather(): lax.ppermute(going_up, axis, [(d, (d + 1) % ways) for d in range(ways)])  39 us
    all_gather x1, blocking collectives, on_device(): lax.all_gather(adapter_up, 'dp', axis=0, tiled=True)  22.9 us
    dynamic_update_slice x8, local copies, waits for them, and re-layouts, ring_gather(): lax.dynamic_update_slice_in_dim(full, going_up, (here - far) % ways * ste...  21.6 us
    all_gather x1, waiting for transfers between devices, on_device(): lax.all_gather(adapter_down, 'dp', axis=0, tiled=True)  21.6 us
    ppermute x7, waiting for transfers between devices, ring_gather(): lax.ppermute(going_down, axis, [(d, (d - 1) % ways) for d in range(ways)])  20.2 us
    dynamic_update_slice x7, local copies, waits for them, and re-layouts, ring_gather(): lax.dynamic_update_slice_in_dim(full, going_down, (here + far) % ways * s...  19.5 us
  transfers between devices with their start and end apart: 18, of which 14 were waited for; matrix products, arithmetic and copies ran while one was open for 15% of the time, Pallas kernels for 0%

profile of v1, /device:TPU:1, one launch (start us, length us, event | category | flops | bytes accessed | tf_op | source)
XLA Modules:
  0.0 422.5 jit_solution(16863313498949463583)
XLA Ops:
  7.2 0.7 all-gather.6.cloned.1.call-update
  8.6 1.7 broadcast_select_fusion
  10.5 0.9 select_reduce_fusion
  11.5 0.2 fusion.8
  11.7 22.9 %all_gather.13 = bf16[128,16,32]{2,1,0:T(8,128)(2,1)S(1)} all-gather(bf16[8,16,32]{2,1,0:T(8,128)(2,1)} %param.12), channel_id=1, replica_groups=mesh['dp'=16,'tensor'=32] {'dp'}, dimensions={0}, use_global_device_ids=true | all-gather | bytes 139264 | tf_op jit(solution)/shard_map/all_gather | solution.py:58
  34.5 0.4 copy.26
  35.0 0.2 convolution_convert_fusion.3
  35.3 21.6 %all-gather.6.cloned.1.call-done = bf16[128,16,256]{2,1,0:T(8,128)(2,1)} async-done(((bf16[8,16,256]{2,1,0:T(8,128)(2,1)}), bf16[128,16,256]{2,1,0:T(8,128)(2,1)}) %all-gather.6.cloned.1.call-update) | async-done | bytes 1048592 | tf_op jit(solution)/shard_map/all_gather | solution.py:57
  56.9 1.6 copy.37
  58.5 0.3 convolution_convert_fusion
  58.9 1.4 convolution_bitcast_fusion
  60.3 103.2 %all-gather.4.cloned.1.call-done = bf16[4096,1024]{1,0:T(8,128)(2,1)} async-done(((bf16[128,1024]{1,0:T(8,128)(2,1)}), bf16[4096,1024]{1,0:T(8,128)(2,1)}) %all-gather.4.cloned.1.call-update) | async-done | bytes 8388624 | tf_op jit(solution)/shard_map/all_gather | solution.py:55
  163.5 1.6 constant_dynamic-slice_fusion
  165.0 1.4 convolution_bitcast_fusion.1
  166.4 117.7 %all-reduce.2 = (bf16[16,32,128]{2,0,1:T(8,128)(2,1)S(1)}, bf16[16,32,128]{2,0,1:T(8,128)(2,1)}) all-reduce(f32[16,32,128]{2,0,1:T(8,128)} %convolution_bitcast_fusion.1, f32[16,32,128]{2,0,1:T(8,128)} %convolution_bitcast_fusion), channel_id=1, replica_groups=mesh['dp'=16,'tensor'=32] {'tensor'}, use_global_device_ids=true, to_apply=%region_1.2 | all-reduce | flops 131072 | bytes 786432 | tf_op jit(solution)/shard_map/psum | solution.py:71
  284.1 0.4 convolution_multiply_fusion.1
  284.5 1.4 convolution_convert_fusion.1
  285.9 2.0 convolution_multiply_fusion.2
  287.9 1.1 copy.31
  289.0 0.3 fusion.5
  289.4 29.5 %collective-permute-start = (bf16[32,16,32]{0,2,1:T(8,128)(2,1)S(1)}, bf16[32,16,32]{0,2,1:T(8,128)(2,1)S(1)}, u32[]{:S(2)}, u32[]{:S(2)}) collective-permute-start(bf16[32,16,32]{0,2,1:T(8,128)(2,1)S(1)} %convert_element_type.37), channel_id=1, source_target_pairs={{0,32},{32,64},{64,96},{96,128},{128,160},{160,192},{192,224},{224... | collective-permute-start | bytes 98312 | tf_op jit(solution)/shard_map/ppermute | solution.py:13
  318.9 1.9 collective-permute-done
  320.9 2.4 collective-permute-start.2
  323.4 2.4 collective-permute-done.2
  325.9 2.5 collective-permute-start.4
  328.4 2.1 collective-permute-done.3
  330.5 0.5 collective-permute-done.4
  331.1 1.8 collective-permute-start.6
  333.0 4.7 %collective-permute-done.5 = bf16[32,16,32]{0,2,1:T(8,128)(2,1)S(1)} collective-permute-done((bf16[32,16,32]{0,2,1:T(8,128)(2,1)S(1)}, bf16[32,16,32]{0,2,1:T(8,128)(2,1)S(1)}, u32[]{:S(2)}, u32[]{:S(2)}) %collective-permute-start.5) | collective-permute-done | bytes 32800 | tf_op jit(solution)/shard_map/ppermute | solution.py:16
  337.7 0.4 collective-permute-start.7
  338.2 1.5 collective-permute-start.8
  339.7 5.2 %collective-permute-done.7 = bf16[32,16,32]{0,2,1:T(8,128)(2,1)S(1)} collective-permute-done((bf16[32,16,32]{0,2,1:T(8,128)(2,1)S(1)}, bf16[32,16,32]{0,2,1:T(8,128)(2,1)S(1)}, u32[]{:S(2)}, u32[]{:S(2)}) %collective-permute-start.7) | collective-permute-done | bytes 32800 | tf_op jit(solution)/shard_map/ppermute | solution.py:16
  344.9 0.6 collective-permute-start.9
  345.5 0.4 collective-permute-done.8
  345.8 0.8 collective-permute-start.10
  346.6 5.8 %collective-permute-done.9 = bf16[32,16,32]{0,2,1:T(8,128)(2,1)} collective-permute-done((bf16[32,16,32]{0,2,1:T(8,128)(2,1)S(1)}, bf16[32,16,32]{0,2,1:T(8,128)(2,1)}, u32[]{:S(2)}, u32[]{:S(2)}) %collective-permute-start.9) | collective-permute-done | bytes 32800 | tf_op jit(solution)/shard_map/ppermute | solution.py:16
  352.4 0.7 collective-permute-start.11
  353.1 0.6 collective-permute-done.10
  353.7 0.4 collective-permute-start.12
  354.2 0.7 convolution_multiply_fusion
  354.9 2.5 collective-permute-done.11
  357.4 1.9 collective-permute-start.13
  359.3 0.4 collective-permute-done.12
  359.7 7.3 %fusion = bf16[4096,256]{1,0:T(8,128)(2,1)} fusion(f32[4096,256]{1,0:T(8,128)S(1)} %bitcast.45, bf16[4096,1024]{1,0:T(8,128)(2,1)} %all-gather.4.cloned.1.call-done, bf16[256,1024]{1,0:T(8,128)(2,1)S(1)} %copy-done.9), kind=kOutput, calls=%fused_computation.1 | convolution fusion | flops 2149580800 | bytes 15204352 | tf_op jit(solution)/shard_map/dot_general | solution.py:74
  367.1 2.9 dynamic_update_slice.48
  370.0 0.6 dynamic_update_slice.49
  370.6 2.9 dynamic_update_slice.50
  373.5 2.8 dynamic_update_slice.51
  376.4 2.9 dynamic_update_slice.52
  379.3 2.8 dynamic_update_slice.53
  382.1 1.4 dynamic_update_slice.54
  383.5 3.6 dynamic_update_slice.55
  387.1 3.7 dynamic_update_slice.56
  390.8 1.5 dynamic_update_slice.57
  392.3 3.7 dynamic_update_slice.58
  396.0 3.7 dynamic_update_slice.59
  399.7 3.7 dynamic_update_slice.60
  403.3 3.7 dynamic_update_slice.61
  407.0 1.4 dynamic_update_slice.62
  408.4 2.9 dynamic_update_slice.63
  411.3 0.5 convolution_convert_fusion.4
  411.8 0.6 copy.33
  412.4 2.9 convolution_convert_fusion.2
  415.3 0.7 copy.32
  (42 shorter events, 1.0 us)
Async XLA Ops:
  7.2 51.7 %copy-start = (bf16[4096,256]{1,0:T(8,128)(2,1)S(1)}, bf16[4096,256]{1,0:T(8,128)(2,1)}, u32[]{:S(2)}) copy-start(bf16[4096,256]{1,0:T(8,128)(2,1)} %param.8) | copy-start | bytes 6291460
  7.2 49.7 %all-gather.6.cloned.1.call-start = ((), (), s32[]{:S(2)}) async-start(), calls=%async_computation.1 | async-start | bytes 1114112 | tf_op jit(solution)/shard_map/all_gather | solution.py:57
  7.9 155.5 %all-gather.4.cloned.1.call-start = ((), (), s32[]{:S(2)}) async-start(), calls=%async_computation | async-start | bytes 8650752 | tf_op jit(solution)/shard_map/all_gather | solution.py:55
  10.4 402.0 %all-gather.8.cloned.1.call-start = ((), (), s32[]{:S(2)}) async-start(), calls=%async_computation.2 | async-start | bytes 4456448 | tf_op jit(solution)/shard_map/all_gather | solution.py:97
  289.4 31.5 %collective-permute-start = (bf16[32,16,32]{0,2,1:T(8,128)(2,1)S(1)}, bf16[32,16,32]{0,2,1:T(8,128)(2,1)S(1)}, u32[]{:S(2)}, u32[]{:S(2)}) collective-permute-start(bf16[32,16,32]{0,2,1:T(8,128)(2,1)S(1)} %convert_element_type.37), channel_id=1, source_target_pairs={{0,32},{32,64},{64,96},{96,128},{128,160},{160,192},{192,224},{224... | collective-permute-start | bytes 98312 | tf_op jit(solution)/shard_map/ppermute | solution.py:13
  318.9 4.4 %collective-permute-start.1 = (bf16[32,16,32]{0,2,1:T(8,128)(2,1)S(1)}, bf16[32,16,32]{0,2,1:T(8,128)(2,1)S(1)}, u32[]{:S(2)}, u32[]{:S(2)}) collective-permute-start(bf16[32,16,32]{0,2,1:T(8,128)(2,1)S(1)} %convert_element_type.37), channel_id=1, source_target_pairs={{0,480},{32,0},{64,32},{96,64},{128,96},{160,128},{192,160},{224,1... | collective-permute-start | bytes 98312 | tf_op jit(solution)/shard_map/ppermute | solution.py:16
  320.9 5.0 %collective-permute-start.2 = (bf16[32,16,32]{0,2,1:T(8,128)(2,1)S(1)}, bf16[32,16,32]{0,2,1:T(8,128)(2,1)S(1)}, u32[]{:S(2)}, u32[]{:S(2)}) collective-permute-start(bf16[32,16,32]{0,2,1:T(8,128)(2,1)S(1)} %collective-permute-done), channel_id=1, source_target_pairs={{0,32},{32,64},{64,96},{96,128},{128,160},{160,192},{192,224},{224... | collective-permute-start | bytes 98312 | tf_op jit(solution)/shard_map/ppermute | solution.py:13
  323.3 7.2 %collective-permute-start.3 = (bf16[32,16,32]{0,2,1:T(8,128)(2,1)S(1)}, bf16[32,16,32]{0,2,1:T(8,128)(2,1)S(1)}, u32[]{:S(2)}, u32[]{:S(2)}) collective-permute-start(bf16[32,16,32]{0,2,1:T(8,128)(2,1)S(1)} %collective-permute-done.1), channel_id=1, source_target_pairs={{0,480},{32,0},{64,32},{96,64},{128,96},{160,128},{192,160},{224,1... | collective-permute-start | bytes 98312 | tf_op jit(solution)/shard_map/ppermute | solution.py:16
  325.9 5.1 %collective-permute-start.4 = (bf16[32,16,32]{0,2,1:T(8,128)(2,1)S(1)}, bf16[32,16,32]{0,2,1:T(8,128)(2,1)S(1)}, u32[]{:S(2)}, u32[]{:S(2)}) collective-permute-start(bf16[32,16,32]{0,2,1:T(8,128)(2,1)S(1)} %collective-permute-done.2), channel_id=1, source_target_pairs={{0,32},{32,64},{64,96},{96,128},{128,160},{160,192},{192,224},{224... | collective-permute-start | bytes 98312 | tf_op jit(solution)/shard_map/ppermute | solution.py:13
  330.5 0.7 copy-start.1
  330.5 7.2 %collective-permute-start.5 = (bf16[32,16,32]{0,2,1:T(8,128)(2,1)S(1)}, bf16[32,16,32]{0,2,1:T(8,128)(2,1)S(1)}, u32[]{:S(2)}, u32[]{:S(2)}) collective-permute-start(bf16[32,16,32]{0,2,1:T(8,128)(2,1)S(1)} %collective-permute-done.3), channel_id=1, source_target_pairs={{0,480},{32,0},{64,32},{96,64},{128,96},{160,128},{192,160},{224,1... | collective-permute-start | bytes 98312 | tf_op jit(solution)/shard_map/ppermute | solution.py:16
  331.1 6.5 %copy-start.3 = (bf16[32,16,32]{0,2,1:T(8,128)(2,1)}, bf16[32,16,32]{0,2,1:T(8,128)(2,1)S(1)}, u32[]{:S(2)}) copy-start(bf16[32,16,32]{0,2,1:T(8,128)(2,1)S(1)} %collective-permute-done.4) | copy-start | bytes 98308
  331.1 7.1 %collective-permute-start.6 = (bf16[32,16,32]{0,2,1:T(8,128)(2,1)S(1)}, bf16[32,16,32]{0,2,1:T(8,128)(2,1)S(1)}, u32[]{:S(2)}, u32[]{:S(2)}) collective-permute-start(bf16[32,16,32]{0,2,1:T(8,128)(2,1)S(1)} %collective-permute-done.4), channel_id=1, source_target_pairs={{0,32},{32,64},{64,96},{96,128},{128,160},{160,192},{192,224},{224... | collective-permute-start | bytes 98312 | tf_op jit(solution)/shard_map/ppermute | solution.py:13
  337.6 22.0 %copy-start.5 = (bf16[32,16,32]{0,2,1:T(8,128)(2,1)}, bf16[32,16,32]{0,2,1:T(8,128)(2,1)S(1)}, u32[]{:S(2)}) copy-start(bf16[32,16,32]{0,2,1:T(8,128)(2,1)S(1)} %collective-permute-done.5) | copy-start | bytes 98308
  337.7 7.2 %collective-permute-start.7 = (bf16[32,16,32]{0,2,1:T(8,128)(2,1)S(1)}, bf16[32,16,32]{0,2,1:T(8,128)(2,1)S(1)}, u32[]{:S(2)}, u32[]{:S(2)}) collective-permute-start(bf16[32,16,32]{0,2,1:T(8,128)(2,1)S(1)} %collective-permute-done.5), channel_id=1, source_target_pairs={{0,480},{32,0},{64,32},{96,64},{128,96},{160,128},{192,160},{224,1... | collective-permute-start | bytes 98312 | tf_op jit(solution)/shard_map/ppermute | solution.py:16
  338.2 21.5 %copy-start.6 = (bf16[32,16,32]{0,2,1:T(8,128)(2,1)}, bf16[32,16,32]{0,2,1:T(8,128)(2,1)S(1)}, u32[]{:S(2)}) copy-start(bf16[32,16,32]{0,2,1:T(8,128)(2,1)S(1)} %collective-permute-done.6) | copy-start | bytes 98308
  338.2 7.6 %collective-permute-start.8 = (bf16[32,16,32]{0,2,1:T(8,128)(2,1)S(1)}, bf16[32,16,32]{0,2,1:T(8,128)(2,1)S(1)}, u32[]{:S(2)}, u32[]{:S(2)}) collective-permute-start(bf16[32,16,32]{0,2,1:T(8,128)(2,1)S(1)} %collective-permute-done.6), channel_id=1, source_target_pairs={{0,32},{32,64},{64,96},{96,128},{128,160},{160,192},{192,224},{224... | collective-permute-start | bytes 98312 | tf_op jit(solution)/shard_map/ppermute | solution.py:13
  344.9 14.8 %copy-start.7 = (bf16[32,16,32]{0,2,1:T(8,128)(2,1)}, bf16[32,16,32]{0,2,1:T(8,128)(2,1)S(1)}, u32[]{:S(2)}) copy-start(bf16[32,16,32]{0,2,1:T(8,128)(2,1)S(1)} %collective-permute-done.7) | copy-start | bytes 98308
  344.9 7.5 %collective-permute-start.9 = (bf16[32,16,32]{0,2,1:T(8,128)(2,1)S(1)}, bf16[32,16,32]{0,2,1:T(8,128)(2,1)}, u32[]{:S(2)}, u32[]{:S(2)}) collective-permute-start(bf16[32,16,32]{0,2,1:T(8,128)(2,1)S(1)} %collective-permute-done.7), channel_id=1, source_target_pairs={{0,480},{32,0},{64,32},{96,64},{128,96},{160,128},{192,160},{224,1... | collective-permute-start | bytes 98312 | tf_op jit(solution)/shard_map/ppermute | solution.py:16
  345.8 13.9 %copy-start.8 = (bf16[32,16,32]{0,2,1:T(8,128)(2,1)}, bf16[32,16,32]{0,2,1:T(8,128)(2,1)S(1)}, u32[]{:S(2)}) copy-start(bf16[32,16,32]{0,2,1:T(8,128)(2,1)S(1)} %collective-permute-done.8) | copy-start | bytes 98308
  345.8 7.9 %collective-permute-start.10 = (bf16[32,16,32]{0,2,1:T(8,128)(2,1)S(1)}, bf16[32,16,32]{0,2,1:T(8,128)(2,1)}, u32[]{:S(2)}, u32[]{:S(2)}) collective-permute-start(bf16[32,16,32]{0,2,1:T(8,128)(2,1)S(1)} %collective-permute-done.8), channel_id=1, source_target_pairs={{0,32},{32,64},{64,96},{96,128},{128,160},{160,192},{192,224},{224... | collective-permute-start | bytes 98312 | tf_op jit(solution)/shard_map/ppermute | solution.py:13
  346.6 13.1 %copy-start.9 = (bf16[256,1024]{1,0:T(8,128)(2,1)S(1)}, bf16[256,1024]{1,0:T(8,128)(2,1)}, u32[]{:S(2)}) copy-start(bf16[256,1024]{1,0:T(8,128)(2,1)} %param.10) | copy-start | bytes 1572868
  352.4 5.0 %collective-permute-start.11 = (bf16[32,16,32]{0,2,1:T(8,128)(2,1)}, bf16[32,16,32]{0,2,1:T(8,128)(2,1)}, u32[]{:S(2)}, u32[]{:S(2)}) collective-permute-start(bf16[32,16,32]{0,2,1:T(8,128)(2,1)} %collective-permute-done.9), channel_id=1, source_target_pairs={{0,480},{32,0},{64,32},{96,64},{128,96},{160,128},{192,160},{224,1... | collective-permute-start | bytes 98312 | tf_op jit(solution)/shard_map/ppermute | solution.py:16
  353.7 5.9 %collective-permute-start.12 = (bf16[32,16,32]{0,2,1:T(8,128)(2,1)}, bf16[32,16,32]{0,2,1:T(8,128)(2,1)}, u32[]{:S(2)}, u32[]{:S(2)}) collective-permute-start(bf16[32,16,32]{0,2,1:T(8,128)(2,1)} %collective-permute-done.10), channel_id=1, source_target_pairs={{0,32},{32,64},{64,96},{96,128},{128,160},{160,192},{192,224},{224... | collective-permute-start | bytes 98312 | tf_op jit(solution)/shard_map/ppermute | solution.py:13
  357.4 49.6 %collective-permute-start.13 = (bf16[32,16,32]{0,2,1:T(8,128)(2,1)}, bf16[32,16,32]{0,2,1:T(8,128)(2,1)}, u32[]{:S(2)}, u32[]{:S(2)}) collective-permute-start(bf16[32,16,32]{0,2,1:T(8,128)(2,1)} %collective-permute-done.11), channel_id=1, source_target_pairs={{0,480},{32,0},{64,32},{96,64},{128,96},{160,128},{192,160},{224,1... | collective-permute-start | bytes 98312 | tf_op jit(solution)/shard_map/ppermute | solution.py:16
  359.7 48.7 %collective-permute-start.14 = (bf16[32,16,32]{0,2,1:T(8,128)(2,1)}, bf16[32,16,32]{0,2,1:T(8,128)(2,1)S(1)}, u32[]{:S(2)}, u32[]{:S(2)}) collective-permute-start(bf16[32,16,32]{0,2,1:T(8,128)(2,1)} %collective-permute-done.12), channel_id=1, source_target_pairs={{0,32},{32,64},{64,96},{96,128},{128,160},{160,192},{192,224},{224... | collective-permute-start | bytes 98312 | tf_op jit(solution)/shard_map/ppermute | solution.py:13
  359.7 16.7 %copy-start.2 = (bf16[32,16,32]{0,2,1:T(8,128)(2,1)S(1)}, bf16[32,16,32]{0,2,1:T(8,128)(2,1)}, u32[]{:S(2)}) copy-start(bf16[32,16,32]{0,2,1:T(8,128)(2,1)} %copy-done.1) | copy-start | bytes 98308
  359.7 19.6 %copy-start.4 = (bf16[32,16,32]{0,2,1:T(8,128)(2,1)S(1)}, bf16[32,16,32]{0,2,1:T(8,128)(2,1)}, u32[]{:S(2)}) copy-start(bf16[32,16,32]{0,2,1:T(8,128)(2,1)} %copy-done.3) | copy-start | bytes 98308
Sparse Core Ops, SparseCore 0:
  10.1 46.6 all-gather.5
  60.6 102.8 all-gather.3
  286.0 71.5 all-gather.7
